TPU v7x, 32 devices: a whole 2x2x4 slice. The times are simulated.
32 devices in a mesh: wide: 8 (over z, y), narrow: 4 (over x, core).
Axes of the slice: x: 2, y: 2, z: 4, core: 2. Of those that a mesh axis runs over, the one named last changes fastest.
Arguments:
- spectra: bfloat16 [512, 2, 8192], P('wide'), may hold values from -6 to 6
- band_gain: float32 [8192], replicated, may hold values from 0.1 to 1.9
- owners: int32 [2], replicated, may hold values from 0 to 7
- pair_near: int32 [8, 2, 512], P('wide', None, 'narrow'), may hold values from 0 to 63
- pair_far: int32 [8, 2, 512], P('wide', None, 'narrow'), may hold values from 0 to 63
- stack_bins: int32 [8, 2, 512], P('wide', None, 'narrow'), may hold values from 0 to 255, as said below
Outputs:
- stacked: float32 [4, 64, 1024], P('narrow', 'wide')
Inputs may be any that keep to these rules, and one draw needn't show every extreme that they name: `stack_bins`: bins n * 64 to (n + 1) * 64 - 1 belong to narrow index n. Of the 256 rows of one device (steps together), at most 128 have bins of one narrow index; in every draw some narrow index gets exactly 128 rows from each device of its group.
All inputs are finite; a program needn't handle non-finite values.
Results may differ from a plain program's by a relative error of at most 0.0036.
Values may be sent and summed in bfloat16 or wider, within the bound.
No kernel may reach another device: no remote copies, remote signals or barrier semaphores. Data moves between devices by JAX's collectives and lax.ppermute only.
A program may use at most 128 MiB of HBM per device.

v0:
```python
import jax
import jax.numpy as jnp
from jax import lax
from jax.sharding import PartitionSpec as P

F = 8192
LAGS = 1024
STEPS = 2
PAIRS = 128
GW = 8


def broadcast(value, axis, root):
    mine = lax.axis_index(axis) == root
    return lax.psum(jnp.where(mine, value, jnp.zeros_like(value)), axis)


def trig_pair(freq_values, lag_values, freqs):
    turns = freq_values[:, None] * lag_values[None, :] % (2 * freqs)
    phase = turns.astype(jnp.float32) * (jnp.pi / freqs)
    return (jnp.cos(phase), jnp.sin(phase))


def lag_table(freqs, lag_count):
    unit_size = 64
    lag_values = jnp.arange(lag_count, dtype=jnp.int32) - lag_count // 2
    coarse_freq = jnp.arange(freqs // unit_size, dtype=jnp.int32) * unit_size
    fine_freq = jnp.arange(unit_size, dtype=jnp.int32)
    coarse_cos, coarse_sin = trig_pair(coarse_freq, lag_values, freqs)
    fine_cos, fine_sin = trig_pair(fine_freq, lag_values, freqs)
    cosine = (
        coarse_cos[:, None, :] * fine_cos[None, :, :]
        - coarse_sin[:, None, :] * fine_sin[None, :, :]
    )
    sine = (
        coarse_sin[:, None, :] * fine_cos[None, :, :]
        + coarse_cos[:, None, :] * fine_sin[None, :, :]
    )
    cosine = cosine.reshape(freqs, lag_count).astype(jnp.bfloat16)
    minus_sine = (-sine).reshape(freqs, lag_count).astype(jnp.bfloat16)
    return jnp.concatenate([cosine, minus_sine], axis=0)


def select_rows(block, indices):
    block_rows = block.shape[0]
    flat_block = block.reshape(block_rows, -1)
    picker = (indices[:, None] == jnp.arange(block_rows, dtype=jnp.int32)[None, :]).astype(
        jnp.bfloat16
    )
    chosen = jnp.dot(picker, flat_block, preferred_element_type=jnp.bfloat16)
    return chosen.reshape(indices.shape[0], 2, -1)


def cross_rows(near_rows, far_rows, band_gain):
    near_real = near_rows[:, 0].astype(jnp.float32)
    near_imag = near_rows[:, 1].astype(jnp.float32)
    far_real = far_rows[:, 0].astype(jnp.float32)
    far_imag = far_rows[:, 1].astype(jnp.float32)
    real_part = (near_real * far_real + near_imag * far_imag) * band_gain
    imag_part = (near_imag * far_real - near_real * far_imag) * band_gain
    return jnp.concatenate([real_part, imag_part], axis=1).astype(jnp.bfloat16)


def local(spectra, band_gain, owners, pair_near, pair_far, stack_bins):
    lag_matrix = lag_table(F, LAGS)
    inv_root = 1.0 / F**0.5
    narrow_count = lax.axis_size("narrow")
    bins_each = GW * lax.axis_size("wide")
    pieces = []
    for step_index in range(STEPS):
        root_index = owners[step_index]
        part_rows = spectra.shape[0] // narrow_count
        own_part = lax.dynamic_slice_in_dim(
            spectra, lax.axis_index("narrow") * part_rows, part_rows, 0
        )
        sent_part = broadcast(own_part, "wide", root_index)
        far_block = lax.all_gather(sent_part, "narrow", axis=0, tiled=True)
        near_rows = select_rows(spectra, pair_near[0, step_index])
        far_rows = select_rows(far_block, pair_far[0, step_index])
        cross_part = cross_rows(near_rows, far_rows, band_gain)
        pieces.append(
            jnp.dot(cross_part, lag_matrix, preferred_element_type=jnp.float32) * inv_root
        )
    lagged = jnp.concatenate(pieces, axis=0)
    bin_ids = stack_bins[0].reshape(-1)
    owner_ids = bin_ids // bins_each
    within = bin_ids % bins_each
    capacity = STEPS * PAIRS // 2
    owner_hits = (owner_ids[:, None] == jnp.arange(narrow_count, dtype=jnp.int32)[None, :]).astype(
        jnp.int32
    )
    ranks = jnp.sum((jnp.cumsum(owner_hits, axis=0) - 1) * owner_hits, axis=1)
    target = owner_ids * capacity + ranks
    outgoing = jnp.zeros((narrow_count * capacity, LAGS), jnp.float32).at[target].set(lagged)
    outgoing = outgoing.reshape(narrow_count, capacity, LAGS)
    slot_bins = jnp.full((narrow_count * capacity,), bins_each, jnp.int32).at[target].set(within)
    slot_bins = slot_bins.reshape(narrow_count, capacity)
    arrived, arrived_bins = (
        lax.all_to_all(outgoing, "narrow", split_axis=0, concat_axis=0, tiled=True),
        lax.all_to_all(slot_bins, "narrow", split_axis=0, concat_axis=0, tiled=True),
    )
    owner_stack = jax.ops.segment_sum(
        arrived.reshape(-1, LAGS), arrived_bins.reshape(-1), num_segments=bins_each + 1
    )[:bins_each]
    stacked = lax.psum_scatter(owner_stack, "wide", scatter_dimension=0, tiled=True)
    stack_scale = (GW / (STEPS * PAIRS)) ** 0.5
    return (stacked * stack_scale)[None]


def solution(mesh):
    in_specs = (
        P("wide", None, None),
        P(),
        P(),
        P("wide", None, "narrow"),
        P("wide", None, "narrow"),
        P("wide", None, "narrow"),
    )
    out_specs = P("narrow", "wide", None)
    return jax.shard_map(local, mesh=mesh, in_specs=in_specs, out_specs=out_specs, check_vma=False)
```

profile of v0, /device:TPU:0, one launch (start us, length us, event | category | flops | bytes accessed | tf_op | source)
XLA Modules:
  0.0 284.0 jit_solution(11070871599337607712)
XLA Ops:
  6.5 1.5 fusion.80
  9.4 2.8 broadcast_select_fusion.1
  12.2 81.1 %all-reduce.3.cloned.1.call-done = (bf16[16,2,8192]{2,1,0:T(2,128)(2,1)}, bf16[16,2,8192]{2,1,0:T(2,128)(2,1)}) async-done(((bf16[16,2,8192]{2,1,0:T(2,128)(2,1)}, bf16[16,2,8192]{2,1,0:T(2,128)(2,1)}), (bf16[16,2,8192]{2,1,0:T(2,128)(2,1)}, bf16[16,2,8192]{2,1,0:T(2,128)(2,1)})) %all-reduce.3.cloned.1.call-update) | async-done | bytes 1048592 | tf_op jit(solution)/shard_map/psum | solution.py:15
  93.3 0.7 and_select_fusion.2
  94.0 1.2 reduce-window.6
  95.3 0.1 slice.68
  95.3 0.1 copy.15
  95.5 0.1 copy.16
  95.6 0.7 and_select_fusion.1
  96.3 0.1 add_bitcast_fusion
  96.4 0.7 compare_select_fusion
  97.1 2.0 scatter_custom_fusion
  99.0 3.2 %all-to-all-start = ((s32[4,1,128]{2,1,0:T(1,128)}), s32[4,1,128]{2,1,0:T(1,128)S(1)}, u32[]{:S(2)}, u32[]{:S(2)}) async-start(s32[4,1,128]{2,1,0:T(1,128)} %bitcast.7), calls=%async_computation | async-start | bytes 4096 | tf_op jit(solution)/shard_map/all_to_all | solution.py:100
  102.3 0.8 slice_bitcast_fusion.2
  103.1 1.7 fusion.61
  104.8 2.1 fusion.56
  107.0 0.0 reduce-scatter.2.cloned.1.call-start
  107.0 5.1 %fusion.30 = bf16[128,2,8192]{2,0,1:T(8,128)(2,1)} fusion(s32[128]{0:T(128)S(1)} %get-tuple-element.22, bf16[8,8,2,8192]{3,2,1,0:T(2,128)(2,1)S(1)} %bitcast.141), kind=kOutput, calls=%fused_computation.44 | convolution fusion | flops 268443648 | bytes 6291968 | tf_op jit(solution)/shard_map/dot_general | solution.py:50
  112.2 5.3 %fusion.32 = bf16[128,2,8192]{2,0,1:T(8,128)(2,1)} fusion(s32[128]{0:T(128)S(1)} %get-tuple-element.21, bf16[8,8,2,8192]{3,2,1,0:T(2,128)(2,1)S(1)} %bitcast.142), kind=kOutput, calls=%fused_computation.46 | convolution fusion | flops 268443648 | bytes 6291968 | tf_op jit(solution)/shard_map/dot_general | solution.py:50
  117.5 14.9 %subtract_convert_fusion = (bf16[128,64,1024]{2,1,0:T(8,128)(2,1)}, bf16[128,64,1024]{2,1,0:T(8,128)(2,1)}) fusion(f32[64,1024]{1,0:T(8,128)S(1)} %copy-done.2, f32[128,1024]{1,0:T(8,128)S(1)} %get-tuple-element.18, f32[64,1024]{1,0:T(8,128)S(1)} %get-tuple-element.19, f32[128,1024]{1,0:T(8,128)S(1)} %get-tuple-element.17), kind=kLoop, calls=%fused_computation.5 | loop fusion | flops 75497472 | bytes 35127296 | tf_op jit(solution)/shard_map/convert_element_type | solution.py:39
  132.3 6.7 %fusion.24 = bf16[128,2,8192]{2,0,1:T(8,128)(2,1)} fusion(s32[128]{0:T(128)S(1)} %get-tuple-element.24, bf16[8,8,2,8192]{3,2,1,0:T(2,128)(2,1)} %bitcast.144), kind=kOutput, calls=%fused_computation.38 | convolution fusion | flops 268443648 | bytes 6291968 | tf_op jit(solution)/shard_map/dot_general | solution.py:50
  139.0 2.3 all-gather.3.cloned.1.call-done
  141.4 4.9 %fusion.27 = bf16[128,2,8192]{2,0,1:T(8,128)(2,1)S(1)} fusion(s32[128]{0:T(128)S(1)} %get-tuple-element.23, bf16[8,8,2,8192]{3,2,1,0:T(2,128)(2,1)} %bitcast.145), kind=kOutput, calls=%fused_computation.41 | convolution fusion | flops 268443648 | bytes 6291968 | tf_op jit(solution)/shard_map/dot_general | solution.py:50
  146.3 6.0 %fusion.5 = (bf16[128,8192]{1,0:T(8,128)(2,1)S(1)}, bf16[128,8192]{1,0:T(8,128)(2,1)S(1)}, bf16[128,8192]{1,0:T(8,128)(2,1)S(1)}, bf16[128,8192]{1,0:T(8,128)(2,1)S(1)}) fusion(f32[8192]{0:T(1024)S(1)} %copy-done.3, bf16[128,2,8192]{2,0,1:T(8,128)(2,1)S(1)} %fusion.27, bf16[128,2,8192]{2,0,1:T(8,128)(2,1)} %fusion.32, bf16[128,2,8192]{2,0,1:T(8,128)(2,1)} %fusion.24, ...), kind=kLoop, calls=%fused_computation.19 | loop fusion | flops 29360128 | bytes 25198592 | tf_op jit(solution)/shard_map/convert.2
  152.4 12.3 %fusion.41 = f32[128,1024]{1,0:T(8,128)S(1)} fusion(bf16[8192,1024]{1,0:T(8,128)(2,1)} %bitcast.139, bf16[8192,1024]{1,0:T(8,128)(2,1)} %bitcast.137, bf16[128,8192]{1,0:T(8,128)(2,1)S(1)} %get-tuple-element.8, bf16[128,8192]{1,0:T(8,128)(2,1)S(1)} %get-tuple-element.7), kind=kOutput, calls=%fused_computation.62 | convolution fusion | flops 4370595840 | bytes 38273024 | tf_op jit(solution)/shard_map/dot_general | solution.py:82
  164.7 12.3 %fusion.44 = f32[128,1024]{1,0:T(8,128)S(1)} fusion(bf16[8192,1024]{1,0:T(8,128)(2,1)} %bitcast.140, bf16[8192,1024]{1,0:T(8,128)(2,1)} %bitcast.138, bf16[128,8192]{1,0:T(8,128)(2,1)S(1)} %get-tuple-element.15, bf16[128,8192]{1,0:T(8,128)(2,1)S(1)} %get-tuple-element.16), kind=kOutput, calls=%fused_computation.63 | convolution fusion | flops 4370595840 | bytes 38273024 | tf_op jit(solution)/shard_map/dot_general | solution.py:82
  176.9 2.2 scatter_custom_fusion.1
  179.2 28.9 %all_to_all.14 = f32[4,128,1024]{2,1,0:T(8,128)} all-to-all(f32[4,128,1024]{2,1,0:T(8,128)S(1)} %bitcast.143), channel_id=1, replica_groups=mesh['wide'=8,'narrow'=4] {'narrow'}, dimensions={0} | all-to-all | bytes 4194304 | tf_op jit(solution)/shard_map/all_to_all | solution.py:99
  208.1 5.8 %scatter_custom_fusion.2 = f32[65,1024]{1,0:T(8,128)S(1)} fusion(s32[512]{0:T(512)S(1)} %bitcast.150, f32[512,1024]{1,0:T(8,128)} %bitcast.146, f32[]{:T(128)} %constant.70.clone.1), kind=kCustom, calls=%fused_computation.78 | custom fusion | flops 524288 | bytes 266752 | tf_op jit(solution)/shard_map/scatter-add | solution.py:102
  213.9 0.7 slice.77
  214.6 61.4 %reduce-scatter.2.cloned.1.call-done = f32[8,1024]{1,0:T(8,128)} async-done(((f32[64,1024]{1,0:T(8,128)}), f32[8,1024]{1,0:T(8,128)}) %reduce-scatter.2.cloned.1.call-update) | async-done | bytes 32784 | tf_op jit(solution)/shard_map/reduce_scatter | solution.py:105
  276.0 1.4 multiply_bitcast_fusion
  (26 shorter events, 0.3 us)
Async XLA Ops:
  6.5 100.5 %copy-start.1 = (bf16[64,2,8192]{2,1,0:T(2,128)(2,1)S(1)}, bf16[64,2,8192]{2,1,0:T(2,128)(2,1)}, u32[]{:S(2)}) copy-start(bf16[64,2,8192]{2,1,0:T(2,128)(2,1)} %param.6) | copy-start | bytes 6291460
  6.5 100.5 %copy-start.4 = (s32[1,2,128]{2,1,0:T(2,128)S(1)}, s32[1,2,128]{2,1,0:T(2,128)}, u32[]{:S(2)}) copy-start(s32[1,2,128]{2,1,0:T(2,128)} %param.9) | copy-start | bytes 3076
  6.5 86.8 %all-reduce.3.cloned.1.call-start = ((), (), s32[]{:S(2)}) async-start(), calls=%async_computation.6 | async-start | bytes 2097152 | tf_op jit(solution)/shard_map/psum | solution.py:15
  12.2 120.1 %all-gather.5.cloned.1.call-start = ((), (), s32[]{:S(2)}) async-start(), calls=%async_computation.4 | async-start | bytes 2621440 | tf_op jit(solution)/shard_map/all_gather | solution.py:77
  99.0 80.1 %all-to-all-start = ((s32[4,1,128]{2,1,0:T(1,128)}), s32[4,1,128]{2,1,0:T(1,128)S(1)}, u32[]{:S(2)}, u32[]{:S(2)}) async-start(s32[4,1,128]{2,1,0:T(1,128)} %bitcast.7), calls=%async_computation | async-start | bytes 4096 | tf_op jit(solution)/shard_map/all_to_all | solution.py:100
  102.3 39.1 %all-gather.3.cloned.1.call-start = ((), (), s32[]{:S(2)}) async-start(), calls=%async_computation.3 | async-start | bytes 2621440 | tf_op jit(solution)/shard_map/all_gather | solution.py:77
  107.0 169.1 %reduce-scatter.2.cloned.1.call-start = ((), (), s32[]{:S(2)}) async-start(), calls=%async_computation.5 | async-start | bytes 294912 | tf_op jit(solution)/shard_map/reduce_scatter | solution.py:105
  112.2 5.3 %copy-start.2 = (f32[64,1024]{1,0:T(8,128)S(1)}, f32[64,1024]{1,0:T(8,128)}, u32[]{:S(2)}) copy-start(f32[64,1024]{1,0:T(8,128)} %get-tuple-element.20) | copy-start | bytes 786436
  139.0 7.3 %copy-start.3 = (f32[8192]{0:T(1024)S(1)}, f32[8192]{0:T(1024)}, u32[]{:S(2)}) copy-start(f32[8192]{0:T(1024)} %param.7) | copy-start | bytes 98308
  141.4 4.9 %copy-start = (bf16[128,2,8192]{2,0,1:T(8,128)(2,1)S(1)}, bf16[128,2,8192]{2,0,1:T(8,128)(2,1)}, u32[]{:S(2)}) copy-start(bf16[128,2,8192]{2,0,1:T(8,128)(2,1)} %fusion.30) | copy-start | bytes 12582916
Sparse Core Ops, SparseCore 0:
  12.3 80.9 all-reduce.2
  95.0 22.1 all-gather.4
  118.8 22.5 all-gather.2
  214.8 61.2 reduce-scatter.1
where the time goes:
time: 284 us
  waiting for transfers between devices  145 us (51%)
  matrix products  46.6 us (16%)
  other arithmetic  40.4 us (14%)
  blocking collectives  28.9 us (10%)
  between operations  14.6 us (5%)
  local copies, waits for them, and re-layouts  5.21 us (2%)
  starting transfers between devices  3.35 us (1%)
    psum x1, waiting for transfers between devices, broadcast(): return lax.psum(jnp.where(mine, value, jnp.zeros_like(value)), axis)  81.1 us
    reduce_scatter x1, waiting for transfers between devices, local(): lax.psum_scatter(owner_stack, 'wide', scatter_dimension=0, tiled=True)  61.4 us
    all_to_all x1, blocking collectives, local(): lax.all_to_all(outgoing, 'narrow', split_axis=0, concat_axis=0, tiled=True)  28.9 us
    dot_general x2, matrix products, local(): jnp.dot(cross_part, lag_matrix, preferred_element_type=jnp.float32)  24.5 us
    dot_general x4, matrix products, select_rows(): chosen = jnp.dot(picker, flat_block, preferred_element_type=jnp.bfloat16)  22 us
    convert_element_type x1, other arithmetic, lag_table(): cosine = cosine.reshape(freqs, lag_count).astype(jnp.bfloat16)  14.9 us
    another operation x3, other arithmetic  7.31 us
    scatter-add x1, other arithmetic, local(): jax.ops.segment_sum(arrived.reshape(-1, LAGS), arrived_bins.reshape(-1),...  5.77 us
  transfers between devices with their start and end apart: 5, of which 3 were waited for; matrix products, arithmetic and copies ran while one was open for 28% of the time, Pallas kernels for 0%

commit v1 on v0

--- a/solution.py
+++ b/solution.py
@@ -12,7 +12,7 @@
 
 def broadcast(value, axis, root):
     mine = lax.axis_index(axis) == root
-    return lax.psum(jnp.where(mine, value, jnp.zeros_like(value)), axis)
+    return jnp.sum(lax.all_gather(jnp.where(mine, value, jnp.zeros_like(value)), axis), axis=0)
 
 
 def trig_pair(freq_values, lag_values, freqs):

time: 284 us -> 358 us (1.26); the launches traced: 284 us -> 352 us
  waiting for transfers between devices: 145 us -> 198 us
  other arithmetic: 40.4 us -> 54.7 us
    all_gather x0 -> x2, waiting for transfers between devices: none -> 130 us  [broadcast(): lax.all_gather(jnp.where(mine, value, jnp.zeros_like(value)), axis)]
    psum x1 -> x0, waiting for transfers between devices: 81.1 us -> none  [broadcast(): return lax.psum(jnp.where(mine, value, jnp.zeros_like(value)), axis)]
    reduce_sum x0 -> x2, other arithmetic: none -> 16.2 us  [broadcast(): jnp.sum(lax.all_gather(jnp.where(mine, value, jnp.zeros_like(value)), axi...]
    all_gather x2, waiting for transfers between devices: 2.34 us -> 6.14 us  [local(): far_block = lax.all_gather(sent_part, 'narrow', axis=0, tiled=True)]
  transfers between devices with their start and end apart: 5 -> 6, of which waited for: 3 -> 4; matrix products, arithmetic and copies ran while one was open for 28% -> 27% of each run, Pallas kernels for 0% -> 0%
where the time goes in v1:
time: 358 us; the launch traced here: 352 us
  waiting for transfers between devices  198 us (55%)
  other arithmetic  54.7 us (15%)
  matrix products  46.6 us (13%)
  blocking collectives  28.9 us (8%)
  between operations  14.9 us (4%)
  local copies, waits for them, and re-layouts  4.36 us (1%)
  starting transfers between devices  3.85 us (1%)
    all_gather x2, waiting for transfers between devices, broadcast(): lax.all_gather(jnp.where(mine, value, jnp.zeros_like(value)), axis)  130 us
    reduce_scatter x1, waiting for transfers between devices, local(): lax.psum_scatter(owner_stack, 'wide', scatter_dimension=0, tiled=True)  61.5 us
    all_to_all x1, blocking collectives, local(): lax.all_to_all(outgoing, 'narrow', split_axis=0, concat_axis=0, tiled=True)  28.9 us
    dot_general x2, matrix products, local(): jnp.dot(cross_part, lag_matrix, preferred_element_type=jnp.float32)  24.5 us
    dot_general x4, matrix products, select_rows(): chosen = jnp.dot(picker, flat_block, preferred_element_type=jnp.bfloat16)  22 us
    reduce_sum x2, other arithmetic, broadcast(): jnp.sum(lax.all_gather(jnp.where(mine, value, jnp.zeros_like(value)), axi...  16.2 us
    convert_element_type x1, other arithmetic, lag_table(): cosine = cosine.reshape(freqs, lag_count).astype(jnp.bfloat16)  15 us
    another operation x3, other arithmetic  7.31 us
  transfers between devices with their start and end apart: 6, of which 4 were waited for; matrix products, arithmetic and copies ran while one was open for 27% of the time, Pallas kernels for 0%

profile of v1, /device:TPU:0, one launch (start us, length us, event | category | flops | bytes accessed | tf_op | source)
XLA Modules:
  0.0 351.5 jit_solution(15237726268495804393)
XLA Ops:
  6.5 1.4 fusion.80
  9.3 2.8 broadcast_select_fusion.1
  12.2 0.7 all-gather.11.cloned.1.call-update
  12.9 75.5 %all-gather.13.cloned.1.call-done = bf16[128,2,8192]{2,1,0:T(2,128)(2,1)} async-done(((bf16[16,2,8192]{2,1,0:T(2,128)(2,1)}), bf16[128,2,8192]{2,1,0:T(2,128)(2,1)}) %all-gather.13.cloned.1.call-update) | async-done | bytes 4194320 | tf_op jit(solution)/shard_map/all_gather | solution.py:15
  88.4 8.1 %reduce_sum.38 = bf16[16,2,8192]{2,1,0:T(2,128)(2,1)} reduce(bf16[8,16,2,8192]{3,2,1,0:T(2,128)(2,1)} %bitcast.147, bf16[]{:T(256)} %constant.86.clone.1), dimensions={0}, to_apply=%region_5.6 | reduce | flops 1835008 | bytes 4718594 | tf_op jit(solution)/shard_map/reduce_sum | solution.py:15
  96.5 1.2 reduce-window.6
  97.8 0.1 slice.68
  97.8 0.1 copy.15
  98.0 0.1 copy.16
  98.1 0.1 add_bitcast_fusion
  98.2 2.0 scatter_custom_fusion
  100.2 3.2 all-to-all-start
  103.4 0.5 all-gather.7.cloned.1.call-start
  103.9 1.8 fusion.61
  105.7 2.1 fusion.56
  107.8 54.4 %all-gather.11.cloned.1.call-done = bf16[128,2,8192]{2,1,0:T(2,128)(2,1)} async-done(((bf16[16,2,8192]{2,1,0:T(2,128)(2,1)}), bf16[128,2,8192]{2,1,0:T(2,128)(2,1)}) %all-gather.11.cloned.1.call-update) | async-done | bytes 4194320 | tf_op jit(solution)/shard_map/all_gather | solution.py:15
  162.2 8.1 %reduce_sum.37 = bf16[16,2,8192]{2,1,0:T(2,128)(2,1)} reduce(bf16[8,16,2,8192]{3,2,1,0:T(2,128)(2,1)} %bitcast.146, bf16[]{:T(256)} %constant.86.clone.1), dimensions={0}, to_apply=%region_4.5 | reduce | flops 1835008 | bytes 4718594 | tf_op jit(solution)/shard_map/reduce_sum | solution.py:15
  170.4 5.1 %fusion.30 = bf16[128,2,8192]{2,0,1:T(8,128)(2,1)} fusion(s32[128]{0:T(128)S(1)} %get-tuple-element.20, bf16[8,8,2,8192]{3,2,1,0:T(2,128)(2,1)S(1)} %bitcast.143), kind=kOutput, calls=%fused_computation.44 | convolution fusion | flops 268443648 | bytes 6291968 | tf_op jit(solution)/shard_map/dot_general | solution.py:50
  175.5 5.3 %fusion.32 = bf16[128,2,8192]{2,0,1:T(8,128)(2,1)} fusion(s32[128]{0:T(128)S(1)} %get-tuple-element.19, bf16[8,8,2,8192]{3,2,1,0:T(2,128)(2,1)S(1)} %bitcast.144), kind=kOutput, calls=%fused_computation.46 | convolution fusion | flops 268443648 | bytes 6291968 | tf_op jit(solution)/shard_map/dot_general | solution.py:50
  180.8 15.0 %subtract_convert_fusion = (bf16[128,64,1024]{2,1,0:T(8,128)(2,1)}, bf16[128,64,1024]{2,1,0:T(8,128)(2,1)}) fusion(f32[64,1024]{1,0:T(8,128)S(1)} %copy-done.2, f32[128,1024]{1,0:T(8,128)S(1)} %get-tuple-element.16, f32[64,1024]{1,0:T(8,128)S(1)} %get-tuple-element.17, f32[128,1024]{1,0:T(8,128)S(1)} %get-tuple-element.15), kind=kLoop, calls=%fused_computation.5 | loop fusion | flops 75497472 | bytes 35127296 | tf_op jit(solution)/shard_map/convert_element_type | solution.py:39
  195.8 6.7 %fusion.24 = bf16[128,2,8192]{2,0,1:T(8,128)(2,1)} fusion(s32[128]{0:T(128)S(1)} %get-tuple-element.22, bf16[8,8,2,8192]{3,2,1,0:T(2,128)(2,1)} %bitcast.148), kind=kOutput, calls=%fused_computation.38 | convolution fusion | flops 268443648 | bytes 6291968 | tf_op jit(solution)/shard_map/dot_general | solution.py:50
  202.5 6.1 %all-gather.7.cloned.1.call-done = bf16[64,2,8192]{2,1,0:T(2,128)(2,1)} async-done(((bf16[16,2,8192]{2,1,0:T(2,128)(2,1)}), bf16[64,2,8192]{2,1,0:T(2,128)(2,1)}) %all-gather.7.cloned.1.call-update) | async-done | bytes 2097168 | tf_op jit(solution)/shard_map/all_gather | solution.py:77
  208.7 4.9 %fusion.27 = bf16[128,2,8192]{2,0,1:T(8,128)(2,1)S(1)} fusion(s32[128]{0:T(128)S(1)} %get-tuple-element.21, bf16[8,8,2,8192]{3,2,1,0:T(2,128)(2,1)} %bitcast.149), kind=kOutput, calls=%fused_computation.41 | convolution fusion | flops 268443648 | bytes 6291968 | tf_op jit(solution)/shard_map/dot_general | solution.py:50
  213.6 6.0 %fusion.5 = (bf16[128,8192]{1,0:T(8,128)(2,1)S(1)}, bf16[128,8192]{1,0:T(8,128)(2,1)S(1)}, bf16[128,8192]{1,0:T(8,128)(2,1)S(1)}, bf16[128,8192]{1,0:T(8,128)(2,1)S(1)}) fusion(f32[8192]{0:T(1024)S(1)} %copy-done.3, bf16[128,2,8192]{2,0,1:T(8,128)(2,1)S(1)} %fusion.27, bf16[128,2,8192]{2,0,1:T(8,128)(2,1)} %fusion.32, bf16[128,2,8192]{2,0,1:T(8,128)(2,1)} %fusion.24, ...), kind=kLoop, calls=%fused_computation.19 | loop fusion | flops 29360128 | bytes 25198592 | tf_op jit(solution)/shard_map/convert.4
  219.7 12.3 %fusion.41 = f32[128,1024]{1,0:T(8,128)S(1)} fusion(bf16[8192,1024]{1,0:T(8,128)(2,1)} %bitcast.141, bf16[8192,1024]{1,0:T(8,128)(2,1)} %bitcast.139, bf16[128,8192]{1,0:T(8,128)(2,1)S(1)} %get-tuple-element.6, bf16[128,8192]{1,0:T(8,128)(2,1)S(1)} %get-tuple-element.5), kind=kOutput, calls=%fused_computation.62 | convolution fusion | flops 4370595840 | bytes 38273024 | tf_op jit(solution)/shard_map/dot_general | solution.py:82
  232.0 12.3 %fusion.44 = f32[128,1024]{1,0:T(8,128)S(1)} fusion(bf16[8192,1024]{1,0:T(8,128)(2,1)} %bitcast.142, bf16[8192,1024]{1,0:T(8,128)(2,1)} %bitcast.140, bf16[128,8192]{1,0:T(8,128)(2,1)S(1)} %get-tuple-element.13, bf16[128,8192]{1,0:T(8,128)(2,1)S(1)} %get-tuple-element.14), kind=kOutput, calls=%fused_computation.63 | convolution fusion | flops 4370595840 | bytes 38273024 | tf_op jit(solution)/shard_map/dot_general | solution.py:82
  244.2 2.2 scatter_custom_fusion.1
  246.5 28.9 %all_to_all.14 = f32[4,128,1024]{2,1,0:T(8,128)} all-to-all(f32[4,128,1024]{2,1,0:T(8,128)S(1)} %bitcast.145), channel_id=1, replica_groups=mesh['wide'=8,'narrow'=4] {'narrow'}, dimensions={0} | all-to-all | bytes 4194304 | tf_op jit(solution)/shard_map/all_to_all | solution.py:99
  275.4 5.8 %scatter_custom_fusion.2 = f32[65,1024]{1,0:T(8,128)S(1)} fusion(s32[512]{0:T(512)S(1)} %bitcast.154, f32[512,1024]{1,0:T(8,128)} %bitcast.150, f32[]{:T(128)} %constant.73.clone.1), kind=kCustom, calls=%fused_computation.78 | custom fusion | flops 524288 | bytes 266752 | tf_op jit(solution)/shard_map/scatter-add | solution.py:102
  281.2 0.7 slice.77
  281.9 61.5 %reduce-scatter.2.cloned.1.call-done = f32[8,1024]{1,0:T(8,128)} async-done(((f32[64,1024]{1,0:T(8,128)}), f32[8,1024]{1,0:T(8,128)}) %reduce-scatter.2.cloned.1.call-update) | async-done | bytes 32784 | tf_op jit(solution)/shard_map/reduce_scatter | solution.py:105
  343.4 1.4 multiply_bitcast_fusion
  (35 shorter events, 0.3 us)
Async XLA Ops:
  6.5 90.0 %copy-start.4 = (s32[1,2,128]{2,1,0:T(2,128)S(1)}, s32[1,2,128]{2,1,0:T(2,128)}, u32[]{:S(2)}) copy-start(s32[1,2,128]{2,1,0:T(2,128)} %param.11) | copy-start | bytes 3076
  6.5 97.4 %copy-start.5 = (s32[1,2,128]{2,1,0:T(2,128)S(1)}, s32[1,2,128]{2,1,0:T(2,128)}, u32[]{:S(2)}) copy-start(s32[1,2,128]{2,1,0:T(2,128)} %param.10) | copy-start | bytes 3076
  6.5 81.8 %all-gather.13.cloned.1.call-start = ((), (), s32[]{:S(2)}) async-start(), calls=%async_computation.7 | async-start | bytes 4718592 | tf_op jit(solution)/shard_map/all_gather | solution.py:15
  12.1 150.1 %all-gather.11.cloned.1.call-start = ((), (), s32[]{:S(2)}) async-start(), calls=%async_computation.6 | async-start | bytes 4718592 | tf_op jit(solution)/shard_map/all_gather | solution.py:15
  12.9 183.0 %all-gather.9.cloned.1.call-start = ((), (), s32[]{:S(2)}) async-start(), calls=%async_computation.4 | async-start | bytes 2621440 | tf_op jit(solution)/shard_map/all_gather | solution.py:77
  96.5 73.9 %copy-start.6 = (s32[1,2,128]{2,1,0:T(2,128)S(1)}, s32[1,2,128]{2,1,0:T(2,128)}, u32[]{:S(2)}) copy-start(s32[1,2,128]{2,1,0:T(2,128)} %param.9) | copy-start | bytes 3076
  96.5 73.9 %copy-start.1 = (bf16[64,2,8192]{2,1,0:T(2,128)(2,1)S(1)}, bf16[64,2,8192]{2,1,0:T(2,128)(2,1)}, u32[]{:S(2)}) copy-start(bf16[64,2,8192]{2,1,0:T(2,128)(2,1)} %param.6) | copy-start | bytes 6291460
  100.2 146.3 %all-to-all-start = ((s32[4,1,128]{2,1,0:T(1,128)}), s32[4,1,128]{2,1,0:T(1,128)S(1)}, u32[]{:S(2)}, u32[]{:S(2)}) async-start(s32[4,1,128]{2,1,0:T(1,128)} %bitcast.7), calls=%async_computation | async-start | bytes 4096 | tf_op jit(solution)/shard_map/all_to_all | solution.py:100
  103.4 105.3 %all-gather.7.cloned.1.call-start = ((), (), s32[]{:S(2)}) async-start(), calls=%async_computation.3 | async-start | bytes 2621440 | tf_op jit(solution)/shard_map/all_gather | solution.py:77
  170.3 173.1 %reduce-scatter.2.cloned.1.call-start = ((), (), s32[]{:S(2)}) async-start(), calls=%async_computation.5 | async-start | bytes 294912 | tf_op jit(solution)/shard_map/reduce_scatter | solution.py:105
  175.5 5.3 %copy-start.2 = (f32[64,1024]{1,0:T(8,128)S(1)}, f32[64,1024]{1,0:T(8,128)}, u32[]{:S(2)}) copy-start(f32[64,1024]{1,0:T(8,128)} %get-tuple-element.18) | copy-start | bytes 786436
  202.5 11.1 %copy-start.3 = (f32[8192]{0:T(1024)S(1)}, f32[8192]{0:T(1024)}, u32[]{:S(2)}) copy-start(f32[8192]{0:T(1024)} %param.7) | copy-start | bytes 98308
  208.7 4.9 %copy-start = (bf16[128,2,8192]{2,0,1:T(8,128)(2,1)S(1)}, bf16[128,2,8192]{2,0,1:T(8,128)(2,1)}, u32[]{:S(2)}) copy-start(bf16[128,2,8192]{2,0,1:T(8,128)(2,1)} %fusion.30) | copy-start | bytes 12582916
Sparse Core Ops, SparseCore 0:
  12.2 76.0 all-gather.12
  90.5 71.6 all-gather.10
  163.7 20.8 all-gather.8
  186.0 22.5 all-gather.6
  282.0 61.2 reduce-scatter.1
